TPU v7x, 128 devices: a whole 4x4x4 slice. The times are simulated.
128 devices in a mesh: req: 16 (over z, x), head: 8 (over y, core).
Axes of the slice: x: 4, y: 4, z: 4, core: 2. Of those that a mesh axis runs over, the one named last changes fastest.
Arguments:
- tokens: bfloat16 [256, 1280], P('req'), may hold values from -6 to 6
- w_qkv: bfloat16 [2, 3, 1280, 1280], P(None, None, 'head'), may hold values from -0.15625 to 0.15625
- w_out: bfloat16 [2, 1280, 1280], P(None, 'head'), may hold values from -0.15625 to 0.15625
- w_up: bfloat16 [2, 1280, 1280], P(None, 'head'), may hold values from -0.15625 to 0.15625
- w_down: bfloat16 [2, 1280, 1280], P(None, 'head'), may hold values from -0.15625 to 0.15625
- gain_attn: float32 [2, 1280], replicated, may hold values from 0.1 to 1.9
- gain_mlp: float32 [2, 1280], replicated, may hold values from 0.1 to 1.9
- suffix_cache: bfloat16 [2, 2, 512, 1280, 128], P(None, None, 'req', 'head'), may hold values from -110 to 110
- prompt_cache: bfloat16 [2, 2, 96, 1280, 128], P(None, None, 'req', 'head'), may hold values from -110 to 110
- suffix_table: int32 [16, 32], P('req'), may hold values from 0 to 31, each once within a row
- prompt_owner: int32 [96], replicated, may hold values from 0 to 95, each once
- suffix_len: int32 [256], P('req'), may hold values from 1 to 256, 32768 in all
- group_id: int32 [256], P('req'), may hold values from 0 to 23, never falling along the last dimension, each value on 1 to 16 neighbouring positions
Outputs:
- hidden: bfloat16 [256, 1280], P('req')
- new_cache: bfloat16 [2, 2, 256, 1280], P(None, None, 'req', 'head')
Inputs may be any that keep to these rules, and one draw needn't show every extreme that they name: `suffix_table`: each row holds every number once. `prompt_owner`: each number once. `group_id`: never falls from one request to the next; every group has 1 to 16 requests, one group exactly 16.
All inputs are finite; a program needn't handle non-finite values. No bound on the sum of `suffix_len` on one device may be relied on, other than what follows from the above.
Results may differ from a plain program's by a relative error of at most 0.019.
The roundings to bfloat16 on the way count: a program that leaves them out, or rounds other values in their place, can miss the bound.
Values may be sent and summed in bfloat16 or wider, within the bound.
No kernel may reach another device: no remote copies, remote signals or barrier semaphores. Data moves between devices by JAX's collectives and lax.ppermute only.
A program may use at most 128 MiB of HBM per device.

v0:
```python
import math
import jax
import jax.numpy as jnp
from jax import lax
from jax.sharding import PartitionSpec as P

HD = 80
PPAGES = 4
NEG_FLOOR = -1e30


def root_norm(values, gains):
    factor = lax.rsqrt(jnp.mean(values * values, axis=-1, keepdims=True) + 1e-06)
    return values * factor * gains


def page_groups(prompt_owner, count, page_len):
    owners = prompt_owner // PPAGES
    return jnp.repeat(owners, page_len, total_repeat_length=count * page_len)


def attend(
    query, key_new, val_new, layer_suffix, layer_prompt, pages, valid, group_id, prompt_owner
):
    row_count = query.shape[0]
    head_count = query.shape[1] // HD
    scale = 1.0 / math.sqrt(HD)
    page_len = layer_suffix.shape[3]
    own_pages = pages.shape[1]
    query_heads = query.reshape(row_count, head_count, HD)
    key_heads = key_new.reshape(row_count, head_count, HD)
    val_heads = val_new.reshape(row_count, head_count, HD)
    gathered_pages = layer_suffix[:, pages].reshape(
        2, row_count, own_pages, head_count, HD, page_len
    )
    scores = (
        jnp.einsum(
            "rhd,rphdt->rhpt", query_heads, gathered_pages[0], preferred_element_type=jnp.float32
        ).reshape(row_count, head_count, own_pages * page_len)
        * scale
    )
    own = (
        jnp.einsum("rhd,rhd->rh", query_heads, key_heads, preferred_element_type=jnp.float32)
        * scale
    )
    mask = valid[:, None, :]
    local_top = jnp.maximum(jnp.max(jnp.where(mask, scores, NEG_FLOOR), axis=-1), own)
    weights = jnp.exp(jnp.where(mask, scores - local_top[..., None], NEG_FLOOR))
    own_weight = jnp.exp(own - local_top)
    total = jnp.sum(weights, axis=-1) + own_weight
    weight_pages = weights.astype(jnp.bfloat16).reshape(row_count, head_count, own_pages, page_len)
    mixed = jnp.einsum(
        "rhpt,rphdt->rhd", weight_pages, gathered_pages[1], preferred_element_type=jnp.float32
    )
    mixed = mixed + jnp.einsum(
        "rh,rhd->rhd",
        own_weight.astype(jnp.bfloat16),
        val_heads,
        preferred_element_type=jnp.float32,
    )
    piece = lax.all_gather(layer_prompt, "req", axis=1, tiled=True)
    count = piece.shape[1]
    key_group = page_groups(prompt_owner, count, page_len)
    keys = piece[0].reshape(count, head_count, HD, page_len)
    vals = piece[1].reshape(count, head_count, HD, page_len)
    block = (
        jnp.einsum("rhd,phdt->rhpt", query_heads, keys, preferred_element_type=jnp.float32).reshape(
            row_count, head_count, count * page_len
        )
        * scale
    )
    match = (group_id[:, None] == key_group[None, :])[:, None, :]
    new_top = jnp.maximum(local_top, jnp.max(jnp.where(match, block, NEG_FLOOR), axis=-1))
    block_weights = jnp.exp(jnp.where(match, block - new_top[..., None], NEG_FLOOR))
    factor = jnp.exp(local_top - new_top)
    new_total = total * factor + jnp.sum(block_weights, axis=-1)
    block_rounded = block_weights.astype(jnp.bfloat16).reshape(
        row_count, head_count, count, page_len
    )
    new_mixed = mixed * factor[..., None] + jnp.einsum(
        "rhpt,phdt->rhd", block_rounded, vals, preferred_element_type=jnp.float32
    )
    return (new_mixed / new_total[..., None]).reshape(row_count, -1).astype(jnp.bfloat16)


def add_branch(residual, partial_value, gains, closing):
    residual = residual + lax.psum(partial_value, "head")
    if closing:
        normed = None
    else:
        normed = root_norm(residual, gains).astype(jnp.bfloat16)
    return (residual, normed)


def local(
    tokens,
    w_qkv,
    w_out,
    w_up,
    w_down,
    gain_attn,
    gain_mlp,
    suffix_cache,
    prompt_cache,
    suffix_table,
    prompt_owner,
    suffix_len,
    group_id,
):
    row_count = tokens.shape[0]
    layer_count = w_qkv.shape[0]
    width_here = w_qkv.shape[2]
    model_width = w_qkv.shape[3]
    pages = suffix_table[0].reshape(row_count, -1)
    span = pages.shape[1] * suffix_cache.shape[4]
    valid = jnp.arange(span, dtype=jnp.int32)[None, :] < suffix_len[:, None]
    whole = tokens.astype(jnp.float32)
    normed = root_norm(whole, gain_attn[0]).astype(jnp.bfloat16)
    residual = whole
    new_keys = []
    new_vals = []
    for layer in range(layer_count):
        projected = jnp.einsum(
            "rd,kd->rk",
            normed,
            w_qkv[layer].reshape(3 * width_here, model_width),
            preferred_element_type=jnp.float32,
        )
        projected = projected.reshape(row_count, 3, width_here).astype(jnp.bfloat16)
        query = projected[:, 0]
        key_new = projected[:, 1]
        val_new = projected[:, 2]
        new_keys.append(key_new)
        new_vals.append(val_new)
        attended = attend(
            query,
            key_new,
            val_new,
            suffix_cache[layer],
            prompt_cache[layer],
            pages,
            valid,
            group_id,
            prompt_owner,
        )
        partial_value = jnp.dot(attended, w_out[layer], preferred_element_type=jnp.float32)
        residual, normed = add_branch(residual, partial_value, gain_mlp[layer], False)
        hidden_units = jax.nn.silu(
            jnp.einsum("rd,fd->rf", normed, w_up[layer], preferred_element_type=jnp.float32)
        ).astype(jnp.bfloat16)
        partial_value = jnp.dot(hidden_units, w_down[layer], preferred_element_type=jnp.float32)
        closing = layer == layer_count - 1
        next_gains = gain_attn[layer] if closing else gain_attn[layer + 1]
        residual, normed = add_branch(residual, partial_value, next_gains, closing)
    hidden = residual.astype(jnp.bfloat16)
    new_cache = jnp.stack([jnp.stack(new_keys), jnp.stack(new_vals)], axis=1)
    return (hidden, new_cache)


def solution(mesh):
    placed = (
        P("req", None),
        P(None, None, "head", None),
        P(None, "head", None),
        P(None, "head", None),
        P(None, "head", None),
        P(),
        P(),
        P(None, None, "req", "head", None),
        P(None, None, "req", "head", None),
        P("req", None),
        P(),
        P("req"),
        P("req"),
    )
    return jax.shard_map(
        local,
        mesh=mesh,
        in_specs=placed,
        out_specs=(P("req", None), P(None, None, "req", "head")),
        check_vma=False,
    )
```

profile of v0, /device:TPU:1, one launch (start us, length us, event | category | flops | bytes accessed | tf_op | source)
XLA Modules:
  0.0 431.9 jit_solution(11187171101283764259)
XLA Ops:
  7.3 2.4 fusion.147
  9.8 0.1 fusion.94
  9.9 0.5 fusion.38
  10.4 0.1 reshape_squeeze.31
  10.7 0.1 fusion.125
  10.8 0.5 broadcast.282
  11.4 0.7 reduce.26
  12.3 73.0 %gather_fusion.2 = s32[12288]{0:T(1024)S(1)} fusion(s32[96]{0:T(128)S(1)} %and_select_fusion, s32[12288]{0:T(1024)S(1)} %fusion.97), kind=kCustom, calls=%fused_computation.clone | custom fusion | bytes 147456 | tf_op jit(solution)/shard_map/jit(_take)/gather | solution.py:19
  85.4 4.6 %slice_bitcast_fusion = (bf16[2,32,160,128]{3,2,1,0:T(8,128)(2,1)S(1)}, bf16[2,32,160,128]{3,2,1,0:T(8,128)(2,1)}) fusion(bf16[2,2,32,160,128]{4,3,2,1,0:T(8,128)(2,1)} %param.26), kind=kLoop, calls=%fused_computation.11 | loop fusion | bytes 10485760 | tf_op jit(solution)/shard_map/squeeze | solution.py:139
  90.0 4.1 gather_fusion
  94.2 1.9 fusion.146
  96.1 0.3 fusion.26
  96.4 0.1 select_reduce_fusion.1
  96.5 0.2 fusion.116
  96.7 0.2 broadcast_compare_fusion
  96.9 0.4 fusion.24
  97.3 3.6 fusion.144
  101.0 0.8 fusion.11
  101.7 0.5 fusion.28
  102.3 1.2 fusion.62
  103.6 1.8 fusion.86
  105.5 0.7 all-gather.7.cloned.1.call-update
  106.3 2.4 gather_fusion.1
  108.8 3.0 fusion.145
  111.8 53.2 %all-reduce.5.cloned.1.call-done = f32[16,1280]{1,0:T(8,128)} async-done(((f32[16,1280]{1,0:T(8,128)}), f32[16,1280]{1,0:T(8,128)}) %all-reduce.5.cloned.1.call-update) | async-done | bytes 81936 | tf_op jit(solution)/shard_map/psum | solution.py:87
  165.0 1.0 multiply_reduce_fusion.2
  166.1 2.2 fusion.82
  168.3 67.2 %all-gather.7.cloned.1.call-done = bf16[1,2,96,160,128]{4,3,2,1,0:T(8,128)(2,1)} async-done(((bf16[1,2,6,160,128]{4,3,2,1,0:T(8,128)(2,1)}), bf16[1,2,96,160,128]{4,3,2,1,0:T(8,128)(2,1)}) %all-gather.7.cloned.1.call-update) | async-done | bytes 7864336 | tf_op jit(solution)/shard_map/all_gather | solution.py:61
  235.5 5.4 %fusion.143 = (bf16[1,1,96,160,128]{4,3,2,1,0:T(8,128)(2,1)}, bf16[1,1,96,160,128]{4,3,2,1,0:T(8,128)(2,1)}) fusion(bf16[1,2,96,160,128]{4,3,2,1,0:T(8,128)(2,1)} %all-gather.7.cloned.1.call-done), kind=kLoop, calls=%fused_computation.177 | loop fusion | bytes 15728640 | tf_op jit(solution)/shard_map/slice | solution.py:64
  241.0 52.7 %all-reduce.7.cloned.1.call-done = f32[16,1280]{1,0:T(8,128)} async-done(((f32[16,1280]{1,0:T(8,128)}), f32[16,1280]{1,0:T(8,128)}) %all-reduce.7.cloned.1.call-update) | async-done | bytes 81936 | tf_op jit(solution)/shard_map/psum | solution.py:87
  293.7 1.0 multiply_reduce_fusion.1
  294.7 1.7 fusion.41
  296.4 0.1 reshape_squeeze.36
  296.7 0.1 fusion.123
  296.9 0.3 fusion.22
  297.2 0.1 select_reduce_fusion
  297.3 0.2 fusion.118
  297.5 2.9 fusion.8
  300.4 1.7 fusion.20
  302.2 0.6 fusion.30
  302.7 3.3 fusion.65
  306.2 1.8 fusion.80
  308.1 56.1 %all-reduce.9.cloned.1.call-done = f32[16,1280]{1,0:T(8,128)} async-done(((f32[16,1280]{1,0:T(8,128)}), f32[16,1280]{1,0:T(8,128)}) %all-reduce.9.cloned.1.call-update) | async-done | bytes 81936 | tf_op jit(solution)/shard_map/psum | solution.py:87
  364.2 1.0 multiply_reduce_fusion
  365.2 2.2 fusion.76
  367.4 0.6 copy.45
  368.0 55.5 %all-reduce.11.cloned.1.call-done = f32[16,1280]{1,0:T(8,128)} async-done(((f32[16,1280]{1,0:T(8,128)}), f32[16,1280]{1,0:T(8,128)}) %all-reduce.11.cloned.1.call-update) | async-done | bytes 81936 | tf_op jit(solution)/shard_map/psum | solution.py:87
  423.5 1.5 add_convert_fusion
  (69 shorter events, 1.7 us)
Async XLA Ops:
  7.2 2.6 copy-start.4
  7.2 2.6 copy-start.2
  7.2 2.7 copy-start.3
  7.2 4.2 copy-start.8
  7.2 90.1 %all-gather.5.cloned.1.call-start = ((), (), s32[]{:S(2)}) async-start(), calls=%async_computation.4 | async-start | bytes 8355840 | tf_op jit(solution)/shard_map/all_gather | solution.py:61
  9.6 2.7 copy-start.9
  9.7 155.4 %all-reduce.5.cloned.1.call-start = ((), (), s32[]{:S(2)}) async-start(), calls=%async_computation | async-start | bytes 163840 | tf_op jit(solution)/shard_map/psum | solution.py:87
  90.0 4.2 copy-start.7
  94.2 2.5 copy-start.6
  105.5 130.1 %all-gather.7.cloned.1.call-start = ((), (), s32[]{:S(2)}) async-start(), calls=%async_computation.5 | async-start | bytes 8355840 | tf_op jit(solution)/shard_map/all_gather | solution.py:61
  106.2 187.5 %all-reduce.7.cloned.1.call-start = ((), (), s32[]{:S(2)}) async-start(), calls=%async_computation.1 | async-start | bytes 163840 | tf_op jit(solution)/shard_map/psum | solution.py:87
  106.2 2.5 copy-start.5
  108.7 57.3 %copy-start = (bf16[2,160,1280]{2,1,0:T(8,128)(2,1)S(1)}, bf16[2,160,1280]{2,1,0:T(8,128)(2,1)}, u32[]{:S(2)}) copy-start(bf16[2,160,1280]{2,1,0:T(8,128)(2,1)} %param.23) | copy-start | bytes 2457604
  168.3 125.4 %copy-start.1 = (f32[16,1280]{1,0:T(8,128)S(1)}, f32[16,1280]{1,0:T(8,128)}, u32[]{:S(2)}) copy-start(f32[16,1280]{1,0:T(8,128)} %all-reduce.5.cloned.1.call-done) | copy-start | bytes 245764
  168.3 195.9 %all-reduce.9.cloned.1.call-start = ((), (), s32[]{:S(2)}) async-start(), calls=%async_computation.2 | async-start | bytes 163840 | tf_op jit(solution)/shard_map/psum | solution.py:87
  308.0 115.5 %all-reduce.11.cloned.1.call-start = ((), (), s32[]{:S(2)}) async-start(), calls=%async_computation.3 | async-start | bytes 163840 | tf_op jit(solution)/shard_map/psum | solution.py:87
Sparse Core Ops, SparseCore 0:
  10.2 71.6 all-gather.4
  105.6 59.4 all-reduce.4
  167.2 68.3 all-gather.6
  237.7 55.9 all-reduce.6
  308.1 55.9 all-reduce.8
  367.5 55.9 all-reduce.10
where the time goes:
time: 433 us; the launch traced here: 432 us
  waiting for transfers between devices  286 us (66%)
  local copies, waits for them, and re-layouts  103 us (24%)
  matrix products  21.1 us (5%)
  between operations  14.4 us (3%)
  other arithmetic  7.59 us (2%)
    psum x4, waiting for transfers between devices, add_branch(): residual = residual + lax.psum(partial_value, 'head')  218 us
    gather x1, local copies, waits for them, and re-layouts, page_groups(): return jnp.repeat(owners, page_len, total_repeat_length=count * page_len)  73 us
    all_gather x2, waiting for transfers between devices, attend(): piece = lax.all_gather(layer_prompt, 'req', axis=1, tiled=True)  67.2 us
    slice x2, local copies, waits for them, and re-layouts, attend(): keys = piece[0].reshape(count, head_count, HD, page_len)  9.05 us
  transfers between devices with their start and end apart: 6, of which 5 were waited for; matrix products, arithmetic and copies ran while one was open for 24% of the time, Pallas kernels for 0%

commit v1 on v0

--- a/solution.py
+++ b/solution.py
@@ -58,7 +58,16 @@
         val_heads,
         preferred_element_type=jnp.float32,
     )
-    piece = lax.all_gather(layer_prompt, "req", axis=1, tiled=True)
+    ways = lax.axis_size("req")
+    up = [(d, (d + 1) % ways) for d in range(ways)]
+    down = [(d, (d - 1) % ways) for d in range(ways)]
+    earlier, later = ([layer_prompt], [layer_prompt])
+    for _ in range(ways // 2):
+        earlier.append(lax.ppermute(earlier[-1], "req", up))
+    for _ in range((ways - 1) // 2):
+        later.append(lax.ppermute(later[-1], "req", down))
+    line = jnp.concatenate([*earlier[::-1], *later[1:]], axis=1)
+    piece = jnp.roll(line, (lax.axis_index("req") - ways // 2) * layer_prompt.shape[1], axis=1)
     count = piece.shape[1]
     key_group = page_groups(prompt_owner, count, page_len)
     keys = piece[0].reshape(count, head_count, HD, page_len)

time: 433 us -> 535 us (1.24)
  starting transfers between devices: 0.24 us -> 68.1 us
  local copies, waits for them, and re-layouts: 103 us -> 120 us
  other arithmetic: 7.59 us -> 16.2 us
  waiting for transfers between devices: 286 us -> 292 us
    ppermute x0 -> x30, starting transfers between devices: none -> 67.8 us  [the longest x14 63.9 us: attend(): later.append(lax.ppermute(later[-1], 'req', down))]
    all_gather x2 -> x0, waiting for transfers between devices: 67.2 us -> none  [attend(): piece = lax.all_gather(layer_prompt, 'req', axis=1, tiled=True)]
    ppermute x0 -> x30, waiting for transfers between devices: none -> 64.2 us  [the longest x16 39.8 us: attend(): earlier.append(lax.ppermute(earlier[-1], 'req', up))]
    unnamed x22 -> x75, local copies, waits for them, and re-layouts: 1.18 us -> 20.8 us
    psum x4, waiting for transfers between devices: 218 us -> 228 us  [add_branch(): residual = residual + lax.psum(partial_value, 'head')]
    concatenate x0 -> x1, other arithmetic: none -> 7.07 us  [attend(): jnp.roll(line, (lax.axis_index('req') - ways // 2) * layer_prompt.shape[1...]
  transfers between devices with their start and end apart: 6 -> 34, of which waited for: 5 -> 18; matrix products, arithmetic and copies ran while one was open for 24% -> 23% of each run, Pallas kernels for 0% -> 0%
where the time goes in v1:
time: 535 us; the launch traced here: 534 us
  waiting for transfers between devices  292 us (55%)
  local copies, waits for them, and re-layouts  120 us (22%)
  starting transfers between devices  68.1 us (13%)
  matrix products  22.6 us (4%)
  other arithmetic  16.2 us (3%)
  between operations  14.3 us (3%)
    psum x4, waiting for transfers between devices, add_branch(): residual = residual + lax.psum(partial_value, 'head')  228 us
    gather x1, local copies, waits for them, and re-layouts, page_groups(): return jnp.repeat(owners, page_len, total_repeat_length=count * page_len)  73 us
    ppermute x14, starting transfers between devices, attend(): later.append(lax.ppermute(later[-1], 'req', down))  63.9 us
    ppermute x16, waiting for transfers between devices, attend(): earlier.append(lax.ppermute(earlier[-1], 'req', up))  39.8 us
    ppermute x14, waiting for transfers between devices, attend(): later.append(lax.ppermute(later[-1], 'req', down))  24.4 us
    unnamed x75, local copies, waits for them, and re-layouts  20.8 us
  transfers between devices with their start and end apart: 34, of which 18 were waited for; matrix products, arithmetic and copies ran while one was open for 23% of the time, Pallas kernels for 0%

profile of v1, /device:TPU:1, one launch (start us, length us, event | category | flops | bytes accessed | tf_op | source)
XLA Modules:
  0.0 533.8 jit_solution(5034129524176053934)
XLA Ops:
  7.2 2.3 slice_bitcast_fusion.2
  9.5 2.0 collective-permute-start
  11.5 4.7 collective-permute-start.8
  16.3 4.8 collective-permute-start.23
  22.8 1.8 fusion.36
  24.6 2.9 collective-permute-done
  29.7 8.4 %collective-permute-done.15 = bf16[2,6,160,128]{3,2,1,0:T(8,128)(2,1)} collective-permute-done((bf16[2,6,160,128]{3,2,1,0:T(8,128)(2,1)}, bf16[2,6,160,128]{3,2,1,0:T(8,128)(2,1)}, u32[]{:S(2)}, u32[]{:S(2)}) %collective-permute-start.15) | collective-permute-done | bytes 491552 | tf_op jit(solution)/shard_map/ppermute | solution.py:66
  38.0 10.5 %collective-permute-done.1 = bf16[2,6,160,128]{3,2,1,0:T(8,128)(2,1)} collective-permute-done((bf16[2,6,160,128]{3,2,1,0:T(8,128)(2,1)S(1)}, bf16[2,6,160,128]{3,2,1,0:T(8,128)(2,1)}, u32[]{:S(2)}, u32[]{:S(2)}) %collective-permute-start.1) | collective-permute-done | bytes 491552 | tf_op jit(solution)/shard_map/ppermute | solution.py:66
  48.6 4.5 slice_bitcast_fusion
  53.1 4.1 gather_fusion
  57.3 4.8 collective-permute-start.9
  63.5 6.1 %collective-permute-done.2 = bf16[2,6,160,128]{3,2,1,0:T(8,128)(2,1)} collective-permute-done((bf16[2,6,160,128]{3,2,1,0:T(8,128)(2,1)}, bf16[2,6,160,128]{3,2,1,0:T(8,128)(2,1)}, u32[]{:S(2)}, u32[]{:S(2)}) %collective-permute-start.2) | collective-permute-done | bytes 491552 | tf_op jit(solution)/shard_map/ppermute | solution.py:66
  69.6 3.0 fusion.118
  72.9 4.8 collective-permute-start.10
  77.7 3.3 collective-permute-done.24
  81.0 5.5 %collective-permute-start.25 = (bf16[2,6,160,128]{3,2,1,0:T(8,128)(2,1)S(1)}, bf16[2,6,160,128]{3,2,1,0:T(8,128)(2,1)}, u32[]{:S(2)}, u32[]{:S(2)}) collective-permute-start(bf16[2,6,160,128]{3,2,1,0:T(8,128)(2,1)S(1)} %collective-permute-done.24), channel_id=1, source_target_pairs={{0,120},{8,0},{16,8},{24,16},{32,24},{40,32},{48,40},{56,48},{64,5... | collective-permute-start | bytes 1474568 | tf_op jit(solution)/shard_map/ppermute | solution.py:68
  86.6 3.8 collective-permute-done.3
  91.6 5.6 %collective-permute-start.11 = (bf16[2,6,160,128]{3,2,1,0:T(8,128)(2,1)}, bf16[2,6,160,128]{3,2,1,0:T(8,128)(2,1)}, u32[]{:S(2)}, u32[]{:S(2)}) collective-permute-start(bf16[2,6,160,128]{3,2,1,0:T(8,128)(2,1)} %collective-permute-done.10), channel_id=1, source_target_pairs={{0,120},{8,0},{16,8},{24,16},{32,24},{40,32},{48,40},{56,48},{64,5... | collective-permute-start | bytes 1474568 | tf_op jit(solution)/shard_map/ppermute | solution.py:68
  97.2 4.9 collective-permute-done.25
  102.1 5.6 %collective-permute-start.26 = (bf16[2,6,160,128]{3,2,1,0:T(8,128)(2,1)}, bf16[2,6,160,128]{3,2,1,0:T(8,128)(2,1)}, u32[]{:S(2)}, u32[]{:S(2)}) collective-permute-start(bf16[2,6,160,128]{3,2,1,0:T(8,128)(2,1)} %collective-permute-done.25), channel_id=1, source_target_pairs={{0,120},{8,0},{16,8},{24,16},{32,24},{40,32},{48,40},{56,48},{64,5... | collective-permute-start | bytes 1474568 | tf_op jit(solution)/shard_map/ppermute | solution.py:68
  108.1 4.6 collective-permute-done.11
  112.7 5.5 %collective-permute-start.12 = (bf16[2,6,160,128]{3,2,1,0:T(8,128)(2,1)}, bf16[2,6,160,128]{3,2,1,0:T(8,128)(2,1)}, u32[]{:S(2)}, u32[]{:S(2)}) collective-permute-start(bf16[2,6,160,128]{3,2,1,0:T(8,128)(2,1)} %collective-permute-done.11), channel_id=1, source_target_pairs={{0,120},{8,0},{16,8},{24,16},{32,24},{40,32},{48,40},{56,48},{64,5... | collective-permute-start | bytes 1474568 | tf_op jit(solution)/shard_map/ppermute | solution.py:68
  118.2 5.0 collective-permute-done.26
  123.3 5.5 %collective-permute-start.27 = (bf16[2,6,160,128]{3,2,1,0:T(8,128)(2,1)}, bf16[2,6,160,128]{3,2,1,0:T(8,128)(2,1)}, u32[]{:S(2)}, u32[]{:S(2)}) collective-permute-start(bf16[2,6,160,128]{3,2,1,0:T(8,128)(2,1)} %collective-permute-done.26), channel_id=1, source_target_pairs={{0,120},{8,0},{16,8},{24,16},{32,24},{40,32},{48,40},{56,48},{64,5... | collective-permute-start | bytes 1474568 | tf_op jit(solution)/shard_map/ppermute | solution.py:68
  129.1 2.4 gather_fusion.1
  131.5 73.0 %gather_fusion.2 = s32[12288]{0:T(1024)S(1)} fusion(s32[96]{0:T(128)S(1)} %and_select_fusion, s32[12288]{0:T(1024)S(1)} %fusion.71), kind=kCustom, calls=%fused_computation.clone | custom fusion | bytes 147456 | tf_op jit(solution)/shard_map/jit(_take)/gather | solution.py:19
  204.6 1.8 fusion.22
  206.4 5.0 collective-permute-start.13
  213.1 1.9 fusion.117
  215.0 2.5 collective-permute-done.13
  217.5 5.1 collective-permute-start.14
  222.6 3.1 collective-permute-done.28
  225.7 5.4 %collective-permute-start.29 = (bf16[2,6,160,128]{3,2,1,0:T(8,128)(2,1)S(1)}, bf16[2,6,160,128]{3,2,1,0:T(8,128)(2,1)S(1)}, u32[]{:S(2)}, u32[]{:S(2)}) collective-permute-start(bf16[2,6,160,128]{3,2,1,0:T(8,128)(2,1)S(1)} %collective-permute-done.28), channel_id=1, source_target_pairs={{0,120},{8,0},{16,8},{24,16},{32,24},{40,32},{48,40},{56,48},{64,5... | collective-permute-start | bytes 1474568 | tf_op jit(solution)/shard_map/ppermute | solution.py:68
  237.9 7.1 %collective-permute-done.22 = bf16[2,6,160,128]{3,2,1,0:T(8,128)(2,1)S(1)} collective-permute-done((bf16[2,6,160,128]{3,2,1,0:T(8,128)(2,1)S(1)}, bf16[2,6,160,128]{3,2,1,0:T(8,128)(2,1)S(1)}, u32[]{:S(2)}, u32[]{:S(2)}) %collective-permute-start.22) | collective-permute-done | bytes 491552 | tf_op jit(solution)/shard_map/ppermute | solution.py:66
  259.2 7.1 %fusion = (bf16[2,96,160,128]{3,2,1,0:T(8,128)(2,1)}, bf16[2,96,160,128]{3,2,1,0:T(8,128)(2,1)S(1)}) fusion(s32[]{:T(128)S(6)} %select_n.90, bf16[2,96,160,128]{3,2,1,0:T(8,128)(2,1)S(1)} %constant_dynamic-update-slice_fusion.16, bf16[2,96,160,128]{3,2,1,0:T(8,128)(2,1)S(1)} %constant_dynamic-update-slice_fusion), kind=kLoop, calls=%fused_computation.7 | loop fusion | flops 7864320 | bytes 31457284 | tf_op jit(solution)/shard_map/jit(_roll_dynamic)/concatenate | solution.py:70
  270.5 66.0 %all-reduce.5.cloned.1.call-done = f32[16,1280]{1,0:T(8,128)} async-done(((f32[16,1280]{1,0:T(8,128)}), f32[16,1280]{1,0:T(8,128)}) %all-reduce.5.cloned.1.call-update) | async-done | bytes 81936 | tf_op jit(solution)/shard_map/psum | solution.py:96
  337.6 2.0 fusion.56
  339.9 5.5 %fusion.115 = (bf16[1,96,160,128]{3,2,1,0:T(8,128)(2,1)}, bf16[1,96,160,128]{3,2,1,0:T(8,128)(2,1)}) fusion(bf16[2,96,160,128]{3,2,1,0:T(8,128)(2,1)} %get-tuple-element.82), kind=kLoop, calls=%fused_computation.207 | loop fusion | bytes 15728640 | tf_op jit(solution)/shard_map/slice | solution.py:73
  345.5 50.3 %all-reduce.7.cloned.1.call-done = f32[16,1280]{1,0:T(8,128)} async-done(((f32[16,1280]{1,0:T(8,128)}), f32[16,1280]{1,0:T(8,128)}) %all-reduce.7.cloned.1.call-update) | async-done | bytes 81936 | tf_op jit(solution)/shard_map/psum | solution.py:96
  396.8 1.7 fusion.39
  399.6 2.9 fusion.6
  403.2 1.7 fusion.18
  404.9 3.3 fusion.47
  408.3 1.8 fusion.54
  410.2 56.1 %all-reduce.9.cloned.1.call-done = f32[16,1280]{1,0:T(8,128)} async-done(((f32[16,1280]{1,0:T(8,128)}), f32[16,1280]{1,0:T(8,128)}) %all-reduce.9.cloned.1.call-update) | async-done | bytes 81936 | tf_op jit(solution)/shard_map/psum | solution.py:96
  467.3 2.3 fusion.50
  470.3 55.5 %all-reduce.11.cloned.1.call-done = f32[16,1280]{1,0:T(8,128)} async-done(((f32[16,1280]{1,0:T(8,128)}), f32[16,1280]{1,0:T(8,128)}) %all-reduce.11.cloned.1.call-update) | async-done | bytes 81936 | tf_op jit(solution)/shard_map/psum | solution.py:96
  525.8 1.5 add_convert_fusion
  (180 shorter events, 40.2 us)
Async XLA Ops:
  7.2 329.4 %all-reduce.5.cloned.1.call-start = ((), (), s32[]{:S(2)}) async-start(), calls=%async_computation | async-start | bytes 163840 | tf_op jit(solution)/shard_map/psum | solution.py:96
  9.5 17.9 %collective-permute-start = (bf16[2,6,160,128]{3,2,1,0:T(8,128)(2,1)}, bf16[2,6,160,128]{3,2,1,0:T(8,128)(2,1)S(1)}, u32[]{:S(2)}, u32[]{:S(2)}) collective-permute-start(bf16[2,6,160,128]{3,2,1,0:T(8,128)(2,1)} %get-tuple-element.63), channel_id=1, source_target_pairs={{0,8},{8,16},{16,24},{24,32},{32,40},{40,48},{48,56},{56,64},{64,7... | collective-permute-start | bytes 1474568 | tf_op jit(solution)/shard_map/ppermute | solution.py:66
  11.5 45.8 %collective-permute-start.8 = (bf16[2,6,160,128]{3,2,1,0:T(8,128)(2,1)}, bf16[2,6,160,128]{3,2,1,0:T(8,128)(2,1)}, u32[]{:S(2)}, u32[]{:S(2)}) collective-permute-start(bf16[2,6,160,128]{3,2,1,0:T(8,128)(2,1)} %get-tuple-element.63), channel_id=1, source_target_pairs={{0,120},{8,0},{16,8},{24,16},{32,24},{40,32},{48,40},{56,48},{64,5... | collective-permute-start | bytes 1474568 | tf_op jit(solution)/shard_map/ppermute | solution.py:68
  16.3 21.8 %collective-permute-start.15 = (bf16[2,6,160,128]{3,2,1,0:T(8,128)(2,1)}, bf16[2,6,160,128]{3,2,1,0:T(8,128)(2,1)}, u32[]{:S(2)}, u32[]{:S(2)}) collective-permute-start(bf16[2,6,160,128]{3,2,1,0:T(8,128)(2,1)} %get-tuple-element.62), channel_id=1, source_target_pairs={{0,8},{8,16},{16,24},{24,32},{32,40},{40,48},{48,56},{56,64},{64,7... | collective-permute-start | bytes 1474568 | tf_op jit(solution)/shard_map/ppermute | solution.py:66
  16.3 45.8 %collective-permute-start.23 = (bf16[2,6,160,128]{3,2,1,0:T(8,128)(2,1)}, bf16[2,6,160,128]{3,2,1,0:T(8,128)(2,1)S(1)}, u32[]{:S(2)}, u32[]{:S(2)}) collective-permute-start(bf16[2,6,160,128]{3,2,1,0:T(8,128)(2,1)} %get-tuple-element.62), channel_id=1, source_target_pairs={{0,120},{8,0},{16,8},{24,16},{32,24},{40,32},{48,40},{56,48},{64,5... | collective-permute-start | bytes 1474568 | tf_op jit(solution)/shard_map/ppermute | solution.py:68
  27.4 21.2 %collective-permute-start.1 = (bf16[2,6,160,128]{3,2,1,0:T(8,128)(2,1)S(1)}, bf16[2,6,160,128]{3,2,1,0:T(8,128)(2,1)}, u32[]{:S(2)}, u32[]{:S(2)}) collective-permute-start(bf16[2,6,160,128]{3,2,1,0:T(8,128)(2,1)S(1)} %collective-permute-done), channel_id=1, source_target_pairs={{0,8},{8,16},{16,24},{24,32},{32,40},{40,48},{48,56},{56,64},{64,7... | collective-permute-start | bytes 1474568 | tf_op jit(solution)/shard_map/ppermute | solution.py:66
  38.0 24.1 %collective-permute-start.16 = (bf16[2,6,160,128]{3,2,1,0:T(8,128)(2,1)}, bf16[2,6,160,128]{3,2,1,0:T(8,128)(2,1)}, u32[]{:S(2)}, u32[]{:S(2)}) collective-permute-start(bf16[2,6,160,128]{3,2,1,0:T(8,128)(2,1)} %collective-permute-done.15), channel_id=1, source_target_pairs={{0,8},{8,16},{16,24},{24,32},{32,40},{40,48},{48,56},{56,64},{64,7... | collective-permute-start | bytes 1474568 | tf_op jit(solution)/shard_map/ppermute | solution.py:66
  48.6 21.1 %collective-permute-start.2 = (bf16[2,6,160,128]{3,2,1,0:T(8,128)(2,1)}, bf16[2,6,160,128]{3,2,1,0:T(8,128)(2,1)}, u32[]{:S(2)}, u32[]{:S(2)}) collective-permute-start(bf16[2,6,160,128]{3,2,1,0:T(8,128)(2,1)} %collective-permute-done.1), channel_id=1, source_target_pairs={{0,8},{8,16},{16,24},{24,32},{32,40},{40,48},{48,56},{56,64},{64,7... | collective-permute-start | bytes 1474568 | tf_op jit(solution)/shard_map/ppermute | solution.py:66
  53.1 37.2 %copy-start.20 = (s32[16]{0:T(128)S(1)}, s32[16]{0:T(128)}, u32[]{:S(2)}) copy-start(s32[16]{0:T(128)} %param.32) | copy-start | bytes 196
  53.1 37.4 %copy-start.21 = (s32[96]{0:T(128)S(1)}, s32[96]{0:T(128)}, u32[]{:S(2)}) copy-start(s32[96]{0:T(128)} %param.31) | copy-start | bytes 1156
  57.3 15.6 %collective-permute-start.9 = (bf16[2,6,160,128]{3,2,1,0:T(8,128)(2,1)}, bf16[2,6,160,128]{3,2,1,0:T(8,128)(2,1)S(1)}, u32[]{:S(2)}, u32[]{:S(2)}) collective-permute-start(bf16[2,6,160,128]{3,2,1,0:T(8,128)(2,1)} %collective-permute-done.8), channel_id=1, source_target_pairs={{0,120},{8,0},{16,8},{24,16},{32,24},{40,32},{48,40},{56,48},{64,5... | collective-permute-start | bytes 1474568 | tf_op jit(solution)/shard_map/ppermute | solution.py:68
  62.1 18.9 %collective-permute-start.24 = (bf16[2,6,160,128]{3,2,1,0:T(8,128)(2,1)S(1)}, bf16[2,6,160,128]{3,2,1,0:T(8,128)(2,1)S(1)}, u32[]{:S(2)}, u32[]{:S(2)}) collective-permute-start(bf16[2,6,160,128]{3,2,1,0:T(8,128)(2,1)S(1)} %collective-permute-done.23), channel_id=1, source_target_pairs={{0,120},{8,0},{16,8},{24,16},{32,24},{40,32},{48,40},{56,48},{64,5... | collective-permute-start | bytes 1474568 | tf_op jit(solution)/shard_map/ppermute | solution.py:68
  62.2 24.4 %collective-permute-start.17 = (bf16[2,6,160,128]{3,2,1,0:T(8,128)(2,1)}, bf16[2,6,160,128]{3,2,1,0:T(8,128)(2,1)S(1)}, u32[]{:S(2)}, u32[]{:S(2)}) collective-permute-start(bf16[2,6,160,128]{3,2,1,0:T(8,128)(2,1)} %collective-permute-done.16), channel_id=1, source_target_pairs={{0,8},{8,16},{16,24},{24,32},{32,40},{40,48},{48,56},{56,64},{64,7... | collective-permute-start | bytes 1474568 | tf_op jit(solution)/shard_map/ppermute | solution.py:66
  69.6 20.7 %collective-permute-start.3 = (bf16[2,6,160,128]{3,2,1,0:T(8,128)(2,1)}, bf16[2,6,160,128]{3,2,1,0:T(8,128)(2,1)S(1)}, u32[]{:S(2)}, u32[]{:S(2)}) collective-permute-start(bf16[2,6,160,128]{3,2,1,0:T(8,128)(2,1)} %collective-permute-done.2), channel_id=1, source_target_pairs={{0,8},{8,16},{16,24},{24,32},{32,40},{40,48},{48,56},{56,64},{64,7... | collective-permute-start | bytes 1474568 | tf_op jit(solution)/shard_map/ppermute | solution.py:66
  72.9 29.2 %copy-start.12 = (bf16[2,6,160,128]{3,2,1,0:T(8,128)(2,1)}, bf16[2,6,160,128]{3,2,1,0:T(8,128)(2,1)S(1)}, u32[]{:S(2)}) copy-start(bf16[2,6,160,128]{3,2,1,0:T(8,128)(2,1)S(1)} %collective-permute-done.9) | copy-start | bytes 1474564
  72.9 18.7 %collective-permute-start.10 = (bf16[2,6,160,128]{3,2,1,0:T(8,128)(2,1)S(1)}, bf16[2,6,160,128]{3,2,1,0:T(8,128)(2,1)}, u32[]{:S(2)}, u32[]{:S(2)}) collective-permute-start(bf16[2,6,160,128]{3,2,1,0:T(8,128)(2,1)S(1)} %collective-permute-done.9), channel_id=1, source_target_pairs={{0,120},{8,0},{16,8},{24,16},{32,24},{40,32},{48,40},{56,48},{64,5... | collective-permute-start | bytes 1474568 | tf_op jit(solution)/shard_map/ppermute | solution.py:68
  81.0 21.1 %collective-permute-start.25 = (bf16[2,6,160,128]{3,2,1,0:T(8,128)(2,1)S(1)}, bf16[2,6,160,128]{3,2,1,0:T(8,128)(2,1)}, u32[]{:S(2)}, u32[]{:S(2)}) collective-permute-start(bf16[2,6,160,128]{3,2,1,0:T(8,128)(2,1)S(1)} %collective-permute-done.24), channel_id=1, source_target_pairs={{0,120},{8,0},{16,8},{24,16},{32,24},{40,32},{48,40},{56,48},{64,5... | collective-permute-start | bytes 1474568 | tf_op jit(solution)/shard_map/ppermute | solution.py:68
  86.5 21.2 %collective-permute-start.18 = (bf16[2,6,160,128]{3,2,1,0:T(8,128)(2,1)S(1)}, bf16[2,6,160,128]{3,2,1,0:T(8,128)(2,1)}, u32[]{:S(2)}, u32[]{:S(2)}) collective-permute-start(bf16[2,6,160,128]{3,2,1,0:T(8,128)(2,1)S(1)} %collective-permute-done.17), channel_id=1, source_target_pairs={{0,8},{8,16},{16,24},{24,32},{32,40},{40,48},{48,56},{56,64},{64,7... | collective-permute-start | bytes 1474568 | tf_op jit(solution)/shard_map/ppermute | solution.py:66
  90.3 17.5 %collective-permute-start.4 = (bf16[2,6,160,128]{3,2,1,0:T(8,128)(2,1)S(1)}, bf16[2,6,160,128]{3,2,1,0:T(8,128)(2,1)}, u32[]{:S(2)}, u32[]{:S(2)}) collective-permute-start(bf16[2,6,160,128]{3,2,1,0:T(8,128)(2,1)S(1)} %collective-permute-done.3), channel_id=1, source_target_pairs={{0,8},{8,16},{16,24},{24,32},{32,40},{40,48},{48,56},{56,64},{64,7... | collective-permute-start | bytes 1474568 | tf_op jit(solution)/shard_map/ppermute | solution.py:66
  91.6 21.2 %collective-permute-start.11 = (bf16[2,6,160,128]{3,2,1,0:T(8,128)(2,1)}, bf16[2,6,160,128]{3,2,1,0:T(8,128)(2,1)}, u32[]{:S(2)}, u32[]{:S(2)}) collective-permute-start(bf16[2,6,160,128]{3,2,1,0:T(8,128)(2,1)} %collective-permute-done.10), channel_id=1, source_target_pairs={{0,120},{8,0},{16,8},{24,16},{32,24},{40,32},{48,40},{56,48},{64,5... | collective-permute-start | bytes 1474568 | tf_op jit(solution)/shard_map/ppermute | solution.py:68
  102.1 21.2 %collective-permute-start.26 = (bf16[2,6,160,128]{3,2,1,0:T(8,128)(2,1)}, bf16[2,6,160,128]{3,2,1,0:T(8,128)(2,1)}, u32[]{:S(2)}, u32[]{:S(2)}) collective-permute-start(bf16[2,6,160,128]{3,2,1,0:T(8,128)(2,1)} %collective-permute-done.25), channel_id=1, source_target_pairs={{0,120},{8,0},{16,8},{24,16},{32,24},{40,32},{48,40},{56,48},{64,5... | collective-permute-start | bytes 1474568 | tf_op jit(solution)/shard_map/ppermute | solution.py:68
  107.7 21.1 %collective-permute-start.19 = (bf16[2,6,160,128]{3,2,1,0:T(8,128)(2,1)}, bf16[2,6,160,128]{3,2,1,0:T(8,128)(2,1)}, u32[]{:S(2)}, u32[]{:S(2)}) collective-permute-start(bf16[2,6,160,128]{3,2,1,0:T(8,128)(2,1)} %collective-permute-done.18), channel_id=1, source_target_pairs={{0,8},{8,16},{16,24},{24,32},{32,40},{40,48},{48,56},{56,64},{64,7... | collective-permute-start | bytes 1474568 | tf_op jit(solution)/shard_map/ppermute | solution.py:66
  107.8 21.0 %collective-permute-start.5 = (bf16[2,6,160,128]{3,2,1,0:T(8,128)(2,1)}, bf16[2,6,160,128]{3,2,1,0:T(8,128)(2,1)}, u32[]{:S(2)}, u32[]{:S(2)}) collective-permute-start(bf16[2,6,160,128]{3,2,1,0:T(8,128)(2,1)} %collective-permute-done.4), channel_id=1, source_target_pairs={{0,8},{8,16},{16,24},{24,32},{32,40},{40,48},{48,56},{56,64},{64,7... | collective-permute-start | bytes 1474568 | tf_op jit(solution)/shard_map/ppermute | solution.py:66
  112.7 93.7 %collective-permute-start.12 = (bf16[2,6,160,128]{3,2,1,0:T(8,128)(2,1)}, bf16[2,6,160,128]{3,2,1,0:T(8,128)(2,1)}, u32[]{:S(2)}, u32[]{:S(2)}) collective-permute-start(bf16[2,6,160,128]{3,2,1,0:T(8,128)(2,1)} %collective-permute-done.11), channel_id=1, source_target_pairs={{0,120},{8,0},{16,8},{24,16},{32,24},{40,32},{48,40},{56,48},{64,5... | collective-permute-start | bytes 1474568 | tf_op jit(solution)/shard_map/ppermute | solution.py:68
  123.3 88.1 %collective-permute-start.27 = (bf16[2,6,160,128]{3,2,1,0:T(8,128)(2,1)}, bf16[2,6,160,128]{3,2,1,0:T(8,128)(2,1)}, u32[]{:S(2)}, u32[]{:S(2)}) collective-permute-start(bf16[2,6,160,128]{3,2,1,0:T(8,128)(2,1)} %collective-permute-done.26), channel_id=1, source_target_pairs={{0,120},{8,0},{16,8},{24,16},{32,24},{40,32},{48,40},{56,48},{64,5... | collective-permute-start | bytes 1474568 | tf_op jit(solution)/shard_map/ppermute | solution.py:68
  128.8 84.0 %collective-permute-start.20 = (bf16[2,6,160,128]{3,2,1,0:T(8,128)(2,1)}, bf16[2,6,160,128]{3,2,1,0:T(8,128)(2,1)}, u32[]{:S(2)}, u32[]{:S(2)}) collective-permute-start(bf16[2,6,160,128]{3,2,1,0:T(8,128)(2,1)} %collective-permute-done.19), channel_id=1, source_target_pairs={{0,8},{8,16},{16,24},{24,32},{32,40},{40,48},{48,56},{56,64},{64,7... | collective-permute-start | bytes 1474568 | tf_op jit(solution)/shard_map/ppermute | solution.py:66
  128.8 84.1 %collective-permute-start.6 = (bf16[2,6,160,128]{3,2,1,0:T(8,128)(2,1)}, bf16[2,6,160,128]{3,2,1,0:T(8,128)(2,1)}, u32[]{:S(2)}, u32[]{:S(2)}) collective-permute-start(bf16[2,6,160,128]{3,2,1,0:T(8,128)(2,1)} %collective-permute-done.5), channel_id=1, source_target_pairs={{0,8},{8,16},{16,24},{24,32},{32,40},{40,48},{48,56},{56,64},{64,7... | collective-permute-start | bytes 1474568 | tf_op jit(solution)/shard_map/ppermute | solution.py:66
  131.5 81.4 %copy-start.19 = (s32[16]{0:T(128)S(1)}, s32[16]{0:T(128)}, u32[]{:S(2)}) copy-start(s32[16]{0:T(128)} %param.33) | copy-start | bytes 196
  131.5 81.6 %copy-start = (bf16[32,2,160,128]{3,2,1,0:T(8,128)(2,1)S(1)}, bf16[32,2,160,128]{3,2,1,0:T(8,128)(2,1)}, u32[]{:S(2)}) copy-start(bf16[32,2,160,128]{3,2,1,0:T(8,128)(2,1)} %gather_fusion.1) | copy-start | bytes 7864324
  204.5 31.0 %copy-start.17 = (bf16[2,6,160,128]{3,2,1,0:T(8,128)(2,1)S(1)}, bf16[2,6,160,128]{3,2,1,0:T(8,128)(2,1)}, u32[]{:S(2)}) copy-start(bf16[2,6,160,128]{3,2,1,0:T(8,128)(2,1)} %copy-done.16) | copy-start | bytes 1474564
  204.6 33.3 %copy-start.9 = (bf16[2,6,160,128]{3,2,1,0:T(8,128)(2,1)S(1)}, bf16[2,6,160,128]{3,2,1,0:T(8,128)(2,1)}, u32[]{:S(2)}) copy-start(bf16[2,6,160,128]{3,2,1,0:T(8,128)(2,1)} %copy-done.8) | copy-start | bytes 1474564
  206.4 11.1 %collective-permute-start.13 = (bf16[2,6,160,128]{3,2,1,0:T(8,128)(2,1)}, bf16[2,6,160,128]{3,2,1,0:T(8,128)(2,1)S(1)}, u32[]{:S(2)}, u32[]{:S(2)}) collective-permute-start(bf16[2,6,160,128]{3,2,1,0:T(8,128)(2,1)} %collective-permute-done.12), channel_id=1, source_target_pairs={{0,120},{8,0},{16,8},{24,16},{32,24},{40,32},{48,40},{56,48},{64,5... | collective-permute-start | bytes 1474568 | tf_op jit(solution)/shard_map/ppermute | solution.py:68
  211.4 14.3 %collective-permute-start.28 = (bf16[2,6,160,128]{3,2,1,0:T(8,128)(2,1)}, bf16[2,6,160,128]{3,2,1,0:T(8,128)(2,1)S(1)}, u32[]{:S(2)}, u32[]{:S(2)}) collective-permute-start(bf16[2,6,160,128]{3,2,1,0:T(8,128)(2,1)} %collective-permute-done.27), channel_id=1, source_target_pairs={{0,120},{8,0},{16,8},{24,16},{32,24},{40,32},{48,40},{56,48},{64,5... | collective-permute-start | bytes 1474568 | tf_op jit(solution)/shard_map/ppermute | solution.py:68
  212.8 18.3 %collective-permute-start.21 = (bf16[2,6,160,128]{3,2,1,0:T(8,128)(2,1)}, bf16[2,6,160,128]{3,2,1,0:T(8,128)(2,1)S(1)}, u32[]{:S(2)}, u32[]{:S(2)}) collective-permute-start(bf16[2,6,160,128]{3,2,1,0:T(8,128)(2,1)} %collective-permute-done.20), channel_id=1, source_target_pairs={{0,8},{8,16},{16,24},{24,32},{32,40},{40,48},{48,56},{56,64},{64,7... | collective-permute-start | bytes 1474568 | tf_op jit(solution)/shard_map/ppermute | solution.py:66
  212.8 19.3 %collective-permute-start.7 = (bf16[2,6,160,128]{3,2,1,0:T(8,128)(2,1)}, bf16[2,6,160,128]{3,2,1,0:T(8,128)(2,1)S(1)}, u32[]{:S(2)}, u32[]{:S(2)}) collective-permute-start(bf16[2,6,160,128]{3,2,1,0:T(8,128)(2,1)} %collective-permute-done.6), channel_id=1, source_target_pairs={{0,8},{8,16},{16,24},{24,32},{32,40},{40,48},{48,56},{56,64},{64,7... | collective-permute-start | bytes 1474568 | tf_op jit(solution)/shard_map/ppermute | solution.py:66
  213.1 35.4 %copy-start.15 = (bf16[2,6,160,128]{3,2,1,0:T(8,128)(2,1)S(1)}, bf16[2,6,160,128]{3,2,1,0:T(8,128)(2,1)}, u32[]{:S(2)}) copy-start(bf16[2,6,160,128]{3,2,1,0:T(8,128)(2,1)} %copy-done.14) | copy-start | bytes 1474564
  215.0 35.8 %copy-start.2 = (bf16[2,2,6,160,128]{4,3,2,1,0:T(8,128)(2,1)S(1)}, bf16[2,2,6,160,128]{4,3,2,1,0:T(8,128)(2,1)}, u32[]{:S(2)}) copy-start(bf16[2,2,6,160,128]{4,3,2,1,0:T(8,128)(2,1)} %param.29) | copy-start | bytes 2949124
  217.5 41.6 %collective-permute-start.14 = (bf16[2,6,160,128]{3,2,1,0:T(8,128)(2,1)S(1)}, bf16[2,6,160,128]{3,2,1,0:T(8,128)(2,1)S(1)}, u32[]{:S(2)}, u32[]{:S(2)}) collective-permute-start(bf16[2,6,160,128]{3,2,1,0:T(8,128)(2,1)S(1)} %collective-permute-done.13), channel_id=1, source_target_pairs={{0,120},{8,0},{16,8},{24,16},{32,24},{40,32},{48,40},{56,48},{64,5... | collective-permute-start | bytes 1474568 | tf_op jit(solution)/shard_map/ppermute | solution.py:68
  225.7 33.4 %collective-permute-start.29 = (bf16[2,6,160,128]{3,2,1,0:T(8,128)(2,1)S(1)}, bf16[2,6,160,128]{3,2,1,0:T(8,128)(2,1)S(1)}, u32[]{:S(2)}, u32[]{:S(2)}) collective-permute-start(bf16[2,6,160,128]{3,2,1,0:T(8,128)(2,1)S(1)} %collective-permute-done.28), channel_id=1, source_target_pairs={{0,120},{8,0},{16,8},{24,16},{32,24},{40,32},{48,40},{56,48},{64,5... | collective-permute-start | bytes 1474568 | tf_op jit(solution)/shard_map/ppermute | solution.py:68
  231.1 13.9 %collective-permute-start.22 = (bf16[2,6,160,128]{3,2,1,0:T(8,128)(2,1)S(1)}, bf16[2,6,160,128]{3,2,1,0:T(8,128)(2,1)S(1)}, u32[]{:S(2)}, u32[]{:S(2)}) collective-permute-start(bf16[2,6,160,128]{3,2,1,0:T(8,128)(2,1)S(1)} %collective-permute-done.21), channel_id=1, source_target_pairs={{0,8},{8,16},{16,24},{24,32},{32,40},{40,48},{48,56},{56,64},{64,7... | collective-permute-start | bytes 1474568 | tf_op jit(solution)/shard_map/ppermute | solution.py:66
  266.8 69.7 %copy-start.7 = (bf16[16,1280]{1,0:T(8,128)(2,1)S(1)}, bf16[16,1280]{1,0:T(8,128)(2,1)}, u32[]{:S(2)}) copy-start(bf16[16,1280]{1,0:T(8,128)(2,1)} %param.21) | copy-start | bytes 122884
  266.8 70.7 %copy-start.3 = (bf16[2,160,1280]{2,1,0:T(8,128)(2,1)S(1)}, bf16[2,160,1280]{2,1,0:T(8,128)(2,1)}, u32[]{:S(2)}) copy-start(bf16[2,160,1280]{2,1,0:T(8,128)(2,1)} %param.25) | copy-start | bytes 2457604
  266.9 70.7 %copy-start.4 = (bf16[2,160,1280]{2,1,0:T(8,128)(2,1)S(1)}, bf16[2,160,1280]{2,1,0:T(8,128)(2,1)}, u32[]{:S(2)}) copy-start(bf16[2,160,1280]{2,1,0:T(8,128)(2,1)} %param.24) | copy-start | bytes 2457604
  270.4 125.4 %all-reduce.7.cloned.1.call-start = ((), (), s32[]{:S(2)}) async-start(), calls=%async_computation.1 | async-start | bytes 163840 | tf_op jit(solution)/shard_map/psum | solution.py:96
  339.6 126.7 %all-reduce.9.cloned.1.call-start = ((), (), s32[]{:S(2)}) async-start(), calls=%async_computation.2 | async-start | bytes 163840 | tf_op jit(solution)/shard_map/psum | solution.py:96
  339.9 55.9 %copy-start.6 = (f32[16,1280]{1,0:T(8,128)S(1)}, f32[16,1280]{1,0:T(8,128)}, u32[]{:S(2)}) copy-start(f32[16,1280]{1,0:T(8,128)} %all-reduce.5.cloned.1.call-done) | copy-start | bytes 245764
  339.9 58.8 %copy-start.1 = (bf16[1,16,2,160,128]{4,3,0,2,1:T(8,128)(2,1)S(1)}, bf16[1,16,2,160,128]{4,3,0,2,1:T(8,128)(2,1)}, u32[]{:S(2)}) copy-start(bf16[1,16,2,160,128]{4,3,0,2,1:T(8,128)(2,1)} %get-tuple-element.53) | copy-start | bytes 3932164
  410.1 115.6 %all-reduce.11.cloned.1.call-start = ((), (), s32[]{:S(2)}) async-start(), calls=%async_computation.3 | async-start | bytes 163840 | tf_op jit(solution)/shard_map/psum | solution.py:96
  (8 other events, 103.7 us)
Sparse Core Ops, SparseCore 0:
  270.5 65.9 all-reduce.4
  339.8 55.9 all-reduce.6
  410.3 55.9 all-reduce.8
  469.7 55.9 all-reduce.10
